TPU v7x, 512 devices: a whole 4x8x8 slice. The times are simulated.
512 devices in a mesh: grp: 16 (over z, core), dev: 32 (over x, y).
Axes of the slice: x: 4, y: 8, z: 8, core: 2. Of those that a mesh axis runs over, the one named last changes fastest.
Arguments:
- ssm_input: bfloat16 [4096, 4096], P('grp', 'dev'), may hold values from -6 to 6
- gate_input: bfloat16 [4096, 4096], P('grp', 'dev'), may hold values from -6 to 6
- step_size: float32 [4096, 64], P('grp', 'dev'), may hold values from 6.1035156e-05 to 0.3375
- decay_rate: float32 [64], P('dev'), may hold values from 0.5 to 2
- in_coeff: bfloat16 [4096, 128], P('grp'), may hold values from -6 to 6
- out_coeff: bfloat16 [4096, 128], P('grp'), may hold values from -6 to 6
- skip_gain: float32 [64], P('dev'), may hold values from 0.5 to 3
- norm_gain: float32 [4096], P('dev'), may hold values from 0.5 to 1.5
- out_proj: bfloat16 [4096, 2048], P(None, 'dev'), may hold values from -0.09375 to 0.09375
- residual: bfloat16 [4096, 2048], P(('grp', 'dev')), may hold values from -6 to 6
- ffn_gain: float32 [2048], replicated, may hold values from 0.5 to 1.5
- router: float32 [2048, 16], replicated, may hold values from -0.125 to 0.125
- routes: int32 [4096, 2], P(('grp', 'dev')), may hold values from 0 to 15, all different within a row; in each aligned block of 8 rows (0 to 7, 8 to 15, ...) at most 2 rows name the same one
- gate_weight: bfloat16 [16, 2048, 8192], P('grp', None, 'dev'), may hold values from -0.125 to 0.125
- up_weight: bfloat16 [16, 2048, 8192], P('grp', None, 'dev'), may hold values from -0.125 to 0.125
- down_weight: bfloat16 [16, 8192, 2048], P('grp', 'dev'), may hold values from -0.0625 to 0.0625
Outputs:
- moe_out: bfloat16 [4096, 2048], P(('grp', 'dev'))
Inputs may be any that keep to these rules, and one draw needn't show every extreme that they name: `routes`: each row names two different experts; among the 8 rows of one dispatch block of consecutive tokens no expert is named more than 2 times, a bound that some block reaches.
All inputs are finite; a program needn't handle non-finite values.
Results may differ from a plain program's by a relative error of at most 0.012.
Values may be sent and summed in bfloat16 or wider, within the bound.
No kernel may reach another device: no remote copies, remote signals or barrier semaphores. Data moves between devices by JAX's collectives and lax.ppermute only.
A program may use at most 64 MiB of HBM per device.

v0:
```python
import jax
import jax.numpy as jnp
from jax import lax
from jax.sharding import Mesh
from jax.sharding import PartitionSpec as P

DEV = ("dev_0", "dev_1")
GRP_DEV = ("grp", "dev_0", "dev_1")
EPSILON = 1e-05
HIGHEST_PREC = lax.Precision.HIGHEST


def side_by_side(arrays, axis, dim, along):
    columns = [a.reshape(*a.shape[:along], -1) for a in arrays]
    both = jnp.concatenate(columns, axis=along)
    filled, at, finished = (lax.all_gather(both, axis, axis=dim, tiled=True), 0, [])
    for a, column in zip(arrays, columns):
        piece = filled[..., at : at + column.shape[along]]
        finished.append(piece.reshape(*piece.shape[:along], *a.shape[along:]))
        at += column.shape[along]
    return tuple(finished)


def sent_to_all(shard, axis):
    peers = lax.axis_size(axis)
    return lax.all_to_all(
        jnp.broadcast_to(shard[None], (peers, *shard.shape)), axis, 0, 0, tiled=True
    )


def of_everyone(shard, axis):
    everything = sent_to_all(shard, axis)
    return jnp.sum(everything, axis=0)


def in_order(tiles, dim):
    dims = list(tiles.shape[1:])
    dims[dim] *= tiles.shape[0]
    return jnp.moveaxis(tiles, 0, dim).reshape(dims)


def collect(shard, axis, dim):
    return in_order(sent_to_all(shard, axis), dim)


def sum_by_axis(terms, axes):
    total = terms.astype(jnp.bfloat16)
    for axis in axes:
        total = lax.psum_scatter(total, axis, scatter_dimension=0, tiled=True)
    return total.astype(jnp.float32)


def ring_gather(shard, axis):
    size = lax.axis_size(axis)
    forward, backward, pieces = (shard, shard, {0: shard})
    for step in range(1, size // 2 + 1):
        forward = lax.ppermute(forward, axis, [(i, (i + 1) % size) for i in range(size)])
        pieces[-step] = forward
        if step < size - step:
            backward = lax.ppermute(backward, axis, [(i, (i - 1) % size) for i in range(size)])
            pieces[step] = backward
    offsets = list(range(-(size // 2), size - size // 2))
    stacked = jnp.stack([pieces[o] for o in offsets])
    doubled = jnp.concatenate([stacked, stacked])
    start = (-offsets[0] - lax.axis_index(axis)) % size
    return lax.dynamic_slice_in_dim(doubled, start, size, 0)


def rms_scale(values, gain_vec):
    return (
        values * lax.rsqrt(jnp.mean(values * values, axis=-1, keepdims=True) + EPSILON) * gain_vec
    )


def slot_tables(routes_block, expert_count, slot_cap):
    blocks, row_total = (routes_block.shape[0], routes_block.shape[1])
    flat_routes = routes_block.reshape(blocks, row_total * 2)
    onehot = (
        flat_routes[:, :, None] == jnp.arange(expert_count, dtype=jnp.int32)[None, None, :]
    ).astype(jnp.int32)
    earlier = jnp.cumsum(onehot, axis=1) - onehot
    slot_rank = jnp.sum(earlier * onehot, axis=2)
    slot_index = (flat_routes * slot_cap + slot_rank).reshape(blocks, row_total, 2)
    placed = (
        slot_index[:, :, :, None]
        == jnp.arange(expert_count * slot_cap, dtype=jnp.int32)[None, None, None, :]
    )
    return placed.astype(jnp.float32)


def shards(
    ssm_input,
    gate_input,
    step_size,
    decay_rate,
    in_coeff,
    out_coeff,
    skip_gain,
    norm_gain,
    out_proj,
    residual,
    ffn_gain,
    router,
    routes,
    gate_weight,
    up_weight,
    down_weight,
):
    tok_rows = ssm_input.shape[0]
    head_count = step_size.shape[1]
    head_width = ssm_input.shape[1] // head_count
    dev_count = lax.axis_size(DEV)
    inner_dim = ssm_input.shape[1] * dev_count
    block_rows = residual.shape[0]
    model_dim = residual.shape[1]
    experts = lax.axis_size("grp")
    slot_cap = max(2, 4 * block_rows // experts)
    group_slots = experts * slot_cap
    inputs_f = ssm_input.astype(jnp.float32).reshape(tok_rows, head_count, head_width)
    in_float = in_coeff.astype(jnp.float32)
    out_float = out_coeff.astype(jnp.float32)
    log_rate = -(step_size * decay_rate[None, :])
    cumulative = jnp.cumsum(log_rate, axis=0)
    causal = (jnp.arange(tok_rows)[:, None] >= jnp.arange(tok_rows)[None, :])[:, :, None]
    spread = cumulative[:, None, :] - cumulative[None, :, :]
    decay_pair = jnp.where(causal, jnp.exp(jnp.where(causal, spread, 0.0)), 0.0)
    scores = jnp.dot(out_coeff, in_coeff.T, preferred_element_type=jnp.float32)
    mixing = decay_pair * scores[:, :, None] * step_size[None, :, :]
    inside = jnp.einsum("tuh,uhp->thp", mixing, inputs_f, precision=HIGHEST_PREC)
    to_end = jnp.exp(cumulative[-1][None, :] - cumulative) * step_size
    own_state = jnp.einsum("uh,uhp,un->hpn", to_end, inputs_f, in_float, precision=HIGHEST_PREC)
    own_log = cumulative[-1]
    group_logs, group_states = tuple(
        (
            part.astype(jnp.float32)
            for part in side_by_side(
                (own_log[None].astype(jnp.bfloat16), own_state[None].astype(jnp.bfloat16)),
                "grp",
                0,
                2,
            )
        )
    )
    group_index = jnp.arange(group_logs.shape[0])
    my_group = lax.axis_index("grp")
    inclusive = jnp.cumsum(group_logs, axis=0)
    exclusive = inclusive - group_logs
    before_me = jnp.sum(jnp.where((group_index == my_group)[:, None], exclusive, 0.0), axis=0)
    earlier_mask = (group_index < my_group)[:, None]
    weighting = jnp.where(
        earlier_mask, jnp.exp(jnp.where(earlier_mask, before_me[None, :] - inclusive, 0.0)), 0.0
    )
    entering = jnp.einsum("gh,ghpn->hpn", weighting, group_states, precision=HIGHEST_PREC)
    carried = jnp.exp(cumulative)[:, :, None] * jnp.einsum(
        "hpn,tn->thp", entering, out_float, precision=HIGHEST_PREC
    )
    ssm_out = inside + carried + skip_gain[None, :, None] * inputs_f
    gated_out = ssm_out.reshape(tok_rows, head_count * head_width) * jax.nn.silu(
        gate_input.astype(jnp.float32)
    )
    gated_gain = gated_out * norm_gain[None, :]
    squares = gated_out * gated_out
    proj_rows = lax.all_to_all(
        out_proj.reshape(dev_count, -1, out_proj.shape[1]), DEV, 0, 0, tiled=True
    )
    chan = proj_rows.shape[1]
    proj_rows = jnp.transpose(proj_rows, (1, 0, 2)).reshape(chan, model_dim)
    lane_pad = 128
    square_cols = (jnp.arange(lane_pad) == 0).astype(jnp.bfloat16)
    rhs = jnp.concatenate(
        [
            jnp.concatenate([proj_rows, jnp.zeros((chan, lane_pad), jnp.bfloat16)], axis=1),
            jnp.concatenate(
                [
                    jnp.zeros((chan, model_dim), jnp.bfloat16),
                    jnp.broadcast_to(square_cols, (chan, lane_pad)),
                ],
                axis=1,
            ),
        ],
        axis=0,
    )
    lhs = jnp.concatenate([gated_gain, squares], axis=1).astype(jnp.bfloat16)
    payload = jnp.dot(lhs, rhs, preferred_element_type=jnp.float32).astype(jnp.bfloat16)
    x_count = lax.axis_size("dev_0")
    y_count = lax.axis_size("dev_1")
    by_x = lax.all_to_all(
        payload.reshape(x_count, y_count, block_rows, payload.shape[1]), "dev_0", 0, 0, tiled=True
    )
    both_weight = jnp.concatenate([gate_weight[0], up_weight[0]], axis=1)
    by_x, both_weight = lax.optimization_barrier((by_x, both_weight))
    by_x = jnp.sum(by_x.astype(jnp.float32), axis=0).astype(jnp.bfloat16)
    landed = lax.all_to_all(by_x, "dev_1", 0, 0, tiled=True)
    landed = jnp.sum(landed.astype(jnp.float32), axis=0)
    summed_proj = landed[:, :model_dim]
    token_squares = landed[:, model_dim]
    mamba_out = (summed_proj * lax.rsqrt(token_squares / inner_dim + EPSILON)[:, None]).astype(
        jnp.bfloat16
    )
    hidden_res = (residual.astype(jnp.float32) + mamba_out.astype(jnp.float32)).astype(jnp.bfloat16)
    hidden_float = hidden_res.astype(jnp.float32)
    normed = rms_scale(hidden_float, ffn_gain).astype(jnp.bfloat16)
    logits = jnp.dot(normed.astype(jnp.float32), router, precision=HIGHEST_PREC)
    expert_ids = jnp.arange(experts, dtype=jnp.int32)[None, :]
    first_logit = jnp.sum(logits * (routes[:, 0:1] == expert_ids).astype(jnp.float32), axis=1)
    second_logit = jnp.sum(logits * (routes[:, 1:2] == expert_ids).astype(jnp.float32), axis=1)
    first_prob = jax.nn.sigmoid(first_logit - second_logit)
    second_prob = 1.0 - first_prob
    placed = slot_tables(routes[None], experts, slot_cap)[0]
    filled = jnp.sum(placed, axis=1)
    outgoing = jnp.dot(
        filled.T.astype(jnp.bfloat16), normed, preferred_element_type=jnp.float32
    ).astype(jnp.bfloat16)
    outgoing = outgoing.reshape(experts, slot_cap, model_dim)
    outgoing = jnp.broadcast_to(outgoing[:, None], (experts, x_count, slot_cap, model_dim))
    arrived = lax.all_to_all(
        outgoing.reshape(experts * x_count, slot_cap, model_dim), ("grp", "dev_0"), 0, 0, tiled=True
    )
    all_rows = lax.all_gather(arrived.reshape(-1, model_dim), "dev_1", axis=0, tiled=True)
    hid_units = gate_weight.shape[2]
    both_act = jnp.dot(all_rows, both_weight, preferred_element_type=jnp.float32)
    hidden = (jax.nn.silu(both_act[:, :hid_units]) * both_act[:, hid_units:]).astype(jnp.bfloat16)
    hidden = lax.optimization_barrier(hidden)
    partial_down = jnp.dot(hidden, down_weight[0], preferred_element_type=jnp.float32)
    summed = lax.psum_scatter(
        partial_down.astype(jnp.bfloat16), "dev_1", scatter_dimension=0, tiled=True
    )
    landed_back = lax.all_to_all(
        summed.reshape(experts * x_count, slot_cap, model_dim), ("grp", "dev_0"), 0, 0, tiled=True
    )
    returned = jnp.sum(
        landed_back.reshape(experts, x_count, slot_cap, model_dim).astype(jnp.float32), axis=1
    )
    weights = first_prob[:, None] * placed[:, 0, :] + second_prob[:, None] * placed[:, 1, :]
    contrib = jnp.dot(weights, returned.reshape(group_slots, model_dim), precision=HIGHEST_PREC)
    return (hidden_float + contrib).astype(jnp.bfloat16)


def solution(mesh):
    torus = Mesh(mesh.devices.reshape(mesh.shape["grp"], 4, 8), ("grp", "dev_0", "dev_1"))
    in_specs = (
        P("grp", DEV),
        P("grp", DEV),
        P("grp", DEV),
        P(DEV),
        P("grp", None),
        P("grp", None),
        P(DEV),
        P(DEV),
        P(None, DEV),
        P(GRP_DEV, None),
        P(),
        P(),
        P(GRP_DEV, None),
        P("grp", None, DEV),
        P("grp", None, DEV),
        P("grp", DEV, None),
    )
    out_specs = P(GRP_DEV, None)
    return jax.shard_map(
        shards, mesh=torus, in_specs=in_specs, out_specs=out_specs, check_vma=False
    )
```

profile of v0, /device:TPU:1, one launch (start us, length us, event | category | flops | bytes accessed | tf_op | source)
XLA Modules:
  0.0 269.2 jit_solution(579986233755267181)
XLA Ops:
  6.5 2.1 copy_bitcast_fusion
  8.6 10.5 %all-to-all-start = ((bf16[32,128,64]{1,2,0:T(8,128)(2,1)}), bf16[32,128,64]{1,2,0:T(8,128)(2,1)S(1)}, u32[]{:S(2)}, u32[]{:S(2)}) async-start(bf16[32,128,64]{1,2,0:T(8,128)(2,1)} %copy_bitcast_fusion), calls=%async_computation | async-start | bytes 1048576 | tf_op jit(solution)/shard_map/all_to_all | solution.py:163
  19.3 0.6 reduce-window.6
  19.9 0.2 slice_reduce_fusion
  20.0 0.2 reduce-window.9
  20.3 0.2 slice_reduce_fusion.1
  20.5 0.1 copy.61
  20.7 0.2 convolution_convert_fusion.3
  21.0 0.1 pad_maximum_fusion.1
  21.1 25.4 %all_gather.6 = bf16[16,2,8193]{2,1,0:T(2,128)(2,1)S(1)} all-gather(bf16[1,2,8193]{2,1,0:T(2,128)(2,1)S(1)} %pad_maximum_fusion.1), channel_id=1, replica_groups=mesh['grp'=16,'dev_0'=4,'dev_1'=8] {'grp'}, dimensions={0}, use_global_device_ids=true | all-gather | bytes 557124 | tf_op jit(solution)/shard_map/all_gather | solution.py:16
  46.5 0.7 slice.56
  47.2 0.1 copy.74
  47.3 0.1 copy.64
  47.5 0.1 select_reduce_fusion.1
  47.7 0.4 reshape.235
  48.1 0.6 fusion.13
  48.7 0.2 fusion.4
  49.0 0.2 fusion.62
  49.2 0.6 fusion.3
  49.8 0.1 copy.66
  50.0 0.3 concatenate.28
  50.3 1.5 convolution_convert_fusion
  51.9 4.4 %all-to-all-start.1 = ((bf16[4,8,8,2176]{3,2,1,0:T(8,128)(2,1)}), bf16[4,8,8,2176]{3,2,1,0:T(8,128)(2,1)S(1)}, u32[]{:S(2)}, u32[]{:S(2)}) async-start(bf16[4,8,8,2176]{3,2,1,0:T(8,128)(2,1)} %bitcast.16), calls=%async_computation.1 | async-start | bytes 2228224 | tf_op jit(solution)/shard_map/all_to_all | solution.py:187
  56.5 2.7 %pad_maximum_fusion = bf16[2048,512]{1,0:T(8,128)(2,1)} fusion(bf16[2048,256]{1,0:T(8,128)(2,1)S(1)} %bitcast.83, bf16[2048,256]{1,0:T(8,128)(2,1)} %bitcast.84), kind=kLoop, calls=%fused_computation.7 | loop fusion | flops 4194304 | bytes 4194304 | tf_op jit(solution)/shard_map/concatenate | solution.py:190
  59.2 12.6 %all-to-all-done.1 = bf16[4,8,8,2176]{3,2,1,0:T(8,128)(2,1)S(1)} async-done(((bf16[4,8,8,2176]{3,2,1,0:T(8,128)(2,1)}), bf16[4,8,8,2176]{3,2,1,0:T(8,128)(2,1)S(1)}, u32[]{:S(2)}, u32[]{:S(2)}) %all-to-all-start.1) | async-done | bytes 1114144 | tf_op jit(solution)/shard_map/all_to_all | solution.py:187
  71.8 0.9 reduce_sum.87
  72.7 6.4 %all-to-all-start.2 = ((bf16[8,8,2176]{2,1,0:T(8,128)(2,1)}), bf16[8,8,2176]{2,1,0:T(8,128)(2,1)S(1)}, u32[]{:S(2)}, u32[]{:S(2)}) async-start(bf16[8,8,2176]{2,1,0:T(8,128)(2,1)} %reduce_sum.87), calls=%async_computation.2 | async-start | bytes 557056 | tf_op jit(solution)/shard_map/all_to_all | solution.py:193
  79.2 0.2 select_reduce_fusion
  79.6 9.8 %all-to-all-done.2 = bf16[8,8,2176]{2,1,0:T(8,128)(2,1)S(1)} async-done(((bf16[8,8,2176]{2,1,0:T(8,128)(2,1)}), bf16[8,8,2176]{2,1,0:T(8,128)(2,1)S(1)}, u32[]{:S(2)}, u32[]{:S(2)}) %all-to-all-start.2) | async-done | bytes 278560 | tf_op jit(solution)/shard_map/all_to_all | solution.py:193
  89.5 0.1 fusion.51
  89.6 0.2 fusion.34
  89.8 0.2 convolution_convert_fusion.2
  90.1 0.1 broadcast_in_dim.78
  90.2 0.3 broadcast_in_dim.79
  90.5 24.0 %all_to_all.25 = bf16[64,2,2048]{2,1,0:T(2,128)(2,1)} all-to-all(bf16[64,2,2048]{2,1,0:T(2,128)(2,1)S(1)} %bitcast.82), channel_id=1, replica_groups=mesh['grp'=16,'dev_0'=4,'dev_1'=8] {'grp','dev_0'}, dimensions={0} | all-to-all | bytes 1048576 | tf_op jit(solution)/shard_map/all_to_all | solution.py:216
  114.5 2.0 reshape.241
  116.6 48.8 %all-gather.2.cloned.1.call-done = bf16[1024,2048]{1,0:T(8,128)(2,1)} async-done(((bf16[128,2048]{1,0:T(8,128)(2,1)}), bf16[1024,2048]{1,0:T(8,128)(2,1)}) %all-gather.2.cloned.1.call-update) | async-done | bytes 4194320 | tf_op jit(solution)/shard_map/all_gather | solution.py:219
  165.4 4.5 %fusion.63 = f32[1024,512]{1,0:T(8,128)S(1)} fusion(bf16[1024,2048]{1,0:T(8,128)(2,1)} %all-gather.2.cloned.1.call-done, bf16[2048,512]{1,0:T(8,128)(2,1)S(1)} %copy-done.1), kind=kOutput, calls=%fused_computation.114 | convolution fusion | flops 2147483648 | bytes 8388608 | tf_op jit(solution)/shard_map/dot_general | solution.py:221
  169.9 0.3 fusion.10
  170.3 3.2 %convolution_convert_fusion.1 = bf16[1024,2048]{1,0:T(8,128)(2,1)} fusion(bf16[1024,256]{1,0:T(8,128)(2,1)S(1)} %fusion.10, bf16[1,256,2048]{2,1,0:T(8,128)(2,1)S(1)} %copy-done), kind=kOutput, calls=%fused_computation.1 | convolution fusion | flops 1075838976 | bytes 5767168 | tf_op jit(solution)/shard_map/dot_general | solution.py:224
  173.5 56.8 %reduce-scatter.2.cloned.1.call-done = bf16[128,2048]{1,0:T(8,128)(2,1)} async-done(((bf16[1024,2048]{1,0:T(8,128)(2,1)}), bf16[128,2048]{1,0:T(8,128)(2,1)}) %reduce-scatter.2.cloned.1.call-update) | async-done | bytes 524304 | tf_op jit(solution)/shard_map/reduce_scatter | solution.py:225
  230.3 2.2 reshape.242
  232.5 11.0 %all-to-all-start.4 = ((bf16[64,2,2048]{2,1,0:T(2,128)(2,1)}), bf16[64,2,2048]{2,1,0:T(2,128)(2,1)S(1)}, u32[]{:S(2)}, u32[]{:S(2)}) async-start(bf16[64,2,2048]{2,1,0:T(2,128)(2,1)} %reshape.242), calls=%async_computation.5 | async-start | bytes 1048576 | tf_op jit(solution)/shard_map/all_to_all | solution.py:228
  243.6 0.3 select_reduce_fusion.2
  244.0 16.8 %all-to-all-done.4 = bf16[64,2,2048]{2,1,0:T(2,128)(2,1)S(1)} async-done(((bf16[64,2,2048]{2,1,0:T(2,128)(2,1)}), bf16[64,2,2048]{2,1,0:T(2,128)(2,1)S(1)}, u32[]{:S(2)}, u32[]{:S(2)}) %all-to-all-start.4) | async-done | bytes 524320 | tf_op jit(solution)/shard_map/all_to_all | solution.py:228
  260.8 0.5 convert_reduce_fusion
  261.2 0.2 reshape.243
  261.4 0.9 fusion.1
  (65 shorter events, 1.5 us)
Async XLA Ops:
  6.5 163.7 %copy-start = (bf16[1,256,2048]{2,1,0:T(8,128)(2,1)S(1)}, bf16[1,256,2048]{2,1,0:T(8,128)(2,1)}, u32[]{:S(2)}) copy-start(bf16[1,256,2048]{2,1,0:T(8,128)(2,1)} %param.31) | copy-start | bytes 3145732
  6.5 12.6 %copy-start.9 = (f32[256,2]{0,1:T(2,128)S(1)}, f32[256,2]{0,1:T(2,128)}, u32[]{:S(2)}) copy-start(f32[256,2]{0,1:T(2,128)} %param.18) | copy-start | bytes 6148
  6.5 12.6 %copy-start.12 = (f32[2]{0:T(128)S(1)}, f32[2]{0:T(128)}, u32[]{:S(2)}) copy-start(f32[2]{0:T(128)} %param.19) | copy-start | bytes 28
  6.5 14.0 %copy-start.6 = (bf16[256,128]{1,0:T(8,128)(2,1)S(1)}, bf16[256,128]{1,0:T(8,128)(2,1)}, u32[]{:S(2)}) copy-start(bf16[256,128]{1,0:T(8,128)(2,1)} %param.16) | copy-start | bytes 196612
  6.5 14.2 %copy-start.3 = (bf16[256,128]{1,0:T(8,128)(2,1)S(1)}, bf16[256,128]{1,0:T(8,128)(2,1)}, u32[]{:S(2)}) copy-start(bf16[256,128]{1,0:T(8,128)(2,1)} %param.20) | copy-start | bytes 196612
  8.6 41.4 %all-to-all-start = ((bf16[32,128,64]{1,2,0:T(8,128)(2,1)}), bf16[32,128,64]{1,2,0:T(8,128)(2,1)S(1)}, u32[]{:S(2)}, u32[]{:S(2)}) async-start(bf16[32,128,64]{1,2,0:T(8,128)(2,1)} %copy_bitcast_fusion), calls=%async_computation | async-start | bytes 1048576 | tf_op jit(solution)/shard_map/all_to_all | solution.py:163
  19.1 29.5 %copy-start.4 = (bf16[256,128]{1,0:T(8,128)(2,1)S(1)}, bf16[256,128]{1,0:T(8,128)(2,1)}, u32[]{:S(2)}) copy-start(bf16[256,128]{1,0:T(8,128)(2,1)} %param.21) | copy-start | bytes 196612
  20.9 28.2 %copy-start.14 = (f32[2]{0:T(128)S(1)}, f32[2]{0:T(128)}, u32[]{:S(2)}) copy-start(f32[2]{0:T(128)} %param.22) | copy-start | bytes 28
  47.2 2.7 %copy-start.5 = (bf16[256,128]{1,0:T(8,128)(2,1)S(1)}, bf16[256,128]{1,0:T(8,128)(2,1)}, u32[]{:S(2)}) copy-start(bf16[256,128]{1,0:T(8,128)(2,1)} %param.17) | copy-start | bytes 196612
  47.2 2.7 copy-start.11
  51.9 4.4 %copy-start.10 = (s32[8,2]{0,1:T(2,128)S(1)}, s32[8,2]{0,1:T(2,128)}, u32[]{:S(2)}) copy-start(s32[8,2]{0,1:T(2,128)} %param.28) | copy-start | bytes 196
  51.9 4.6 %copy-start.2 = (bf16[1,2048,256]{2,1,0:T(8,128)(2,1)S(1)}, bf16[1,2048,256]{2,1,0:T(8,128)(2,1)}, u32[]{:S(2)}) copy-start(bf16[1,2048,256]{2,1,0:T(8,128)(2,1)} %param.30) | copy-start | bytes 3145732
  51.9 19.9 %all-to-all-start.1 = ((bf16[4,8,8,2176]{3,2,1,0:T(8,128)(2,1)}), bf16[4,8,8,2176]{3,2,1,0:T(8,128)(2,1)S(1)}, u32[]{:S(2)}, u32[]{:S(2)}) async-start(bf16[4,8,8,2176]{3,2,1,0:T(8,128)(2,1)} %bitcast.16), calls=%async_computation.1 | async-start | bytes 2228224 | tf_op jit(solution)/shard_map/all_to_all | solution.py:187
  59.2 30.4 %copy-start.7 = (bf16[8,2048]{1,0:T(8,128)(2,1)S(1)}, bf16[8,2048]{1,0:T(8,128)(2,1)}, u32[]{:S(2)}) copy-start(bf16[8,2048]{1,0:T(8,128)(2,1)} %param.25) | copy-start | bytes 98308
  59.2 30.6 %copy-start.8 = (f32[2048]{0:T(1024)S(1)}, f32[2048]{0:T(1024)}, u32[]{:S(2)}) copy-start(f32[2048]{0:T(1024)} %param.26) | copy-start | bytes 24580
  72.7 16.8 %all-to-all-start.2 = ((bf16[8,8,2176]{2,1,0:T(8,128)(2,1)}), bf16[8,8,2176]{2,1,0:T(8,128)(2,1)S(1)}, u32[]{:S(2)}, u32[]{:S(2)}) async-start(bf16[8,8,2176]{2,1,0:T(8,128)(2,1)} %reduce_sum.87), calls=%async_computation.2 | async-start | bytes 557056 | tf_op jit(solution)/shard_map/all_to_all | solution.py:193
  79.0 86.4 %all-gather.2.cloned.1.call-start = ((), (), s32[]{:S(2)}) async-start(), calls=%async_computation.6 | async-start | bytes 4718592 | tf_op jit(solution)/shard_map/all_gather | solution.py:219
  79.6 85.8 %copy-start.1 = (bf16[2048,512]{1,0:T(8,128)(2,1)S(1)}, bf16[2048,512]{1,0:T(8,128)(2,1)}, u32[]{:S(2)}) copy-start(bf16[2048,512]{1,0:T(8,128)(2,1)} %pad_maximum_fusion) | copy-start | bytes 6291460
  116.6 113.8 %reduce-scatter.2.cloned.1.call-start = ((), (), s32[]{:S(2)}) async-start(), calls=%async_computation.7 | async-start | bytes 4718592 | tf_op jit(solution)/shard_map/reduce_scatter | solution.py:225
  173.5 70.1 %copy-start.13 = (f32[2048,16]{0,1:T(8,128)S(1)}, f32[2048,16]{0,1:T(8,128)}, u32[]{:S(2)}) copy-start(f32[2048,16]{0,1:T(8,128)} %param.27) | copy-start | bytes 393220
  232.5 28.2 %all-to-all-start.4 = ((bf16[64,2,2048]{2,1,0:T(2,128)(2,1)}), bf16[64,2,2048]{2,1,0:T(2,128)(2,1)S(1)}, u32[]{:S(2)}, u32[]{:S(2)}) async-start(bf16[64,2,2048]{2,1,0:T(2,128)(2,1)} %reshape.242), calls=%async_computation.5 | async-start | bytes 1048576 | tf_op jit(solution)/shard_map/all_to_all | solution.py:228
Sparse Core Ops, SparseCore 0:
  116.7 48.6 all-gather.1
  173.6 56.6 reduce-scatter.1
where the time goes:
time: 270 us; the launch traced here: 269 us
  waiting for transfers between devices  145 us (54%)
  blocking collectives  49.4 us (18%)
  starting transfers between devices  32.3 us (12%)
  between operations  13.8 us (5%)
  matrix products  12.5 us (5%)
  local copies, waits for them, and re-layouts  9.64 us (4%)
  other arithmetic  6.72 us (2%)
    reduce_scatter x1, waiting for transfers between devices, shards(): lax.psum_scatter(partial_down.astype(jnp.bfloat16), 'dev_1', scatter_dime...  56.8 us
    all_gather x1, waiting for transfers between devices, shards(): lax.all_gather(arrived.reshape(-1, model_dim), 'dev_1', axis=0, tiled=True)  48.8 us
    all_gather x1, blocking collectives, side_by_side(): lax.all_gather(both, axis, axis=dim, tiled=True)  25.4 us
    all_to_all x1, blocking collectives, shards(): lax.all_to_all(outgoing.reshape(experts * x_count, slot_cap, model_dim),...  24 us
    all_to_all x1, waiting for transfers between devices, shards(): lax.all_to_all(summed.reshape(experts * x_count, slot_cap, model_dim), ('...  16.8 us
    all_to_all x1, waiting for transfers between devices, shards(): lax.all_to_all(payload.reshape(x_count, y_count, block_rows, payload.shap...  12.6 us
    all_to_all x1, starting transfers between devices, shards(): lax.all_to_all(summed.reshape(experts * x_count, slot_cap, model_dim), ('...  11 us
    all_to_all x1, starting transfers between devices, shards(): lax.all_to_all(out_proj.reshape(dev_count, -1, out_proj.shape[1]), DEV, 0...  10.5 us
  transfers between devices with their start and end apart: 6, of which 5 were waited for; matrix products, arithmetic and copies ran while one was open for 3% of the time, Pallas kernels for 0%

commit v1 on v0

--- a/solution.py
+++ b/solution.py
@@ -8,6 +8,13 @@
 GRP_DEV = ("grp", "dev_0", "dev_1")
 EPSILON = 1e-05
 HIGHEST_PREC = lax.Precision.HIGHEST
+
+
+def exchange_gather(block, axis, dim):
+    n_dev = lax.axis_size(axis)
+    parts = jnp.stack([block for _ in range(n_dev)])
+    parts = lax.all_to_all(parts, axis, split_axis=0, concat_axis=0)
+    return jnp.concatenate(parts, axis=dim)
 
 
 def side_by_side(arrays, axis, dim, along):
@@ -216,7 +223,7 @@
     arrived = lax.all_to_all(
         outgoing.reshape(experts * x_count, slot_cap, model_dim), ("grp", "dev_0"), 0, 0, tiled=True
     )
-    all_rows = lax.all_gather(arrived.reshape(-1, model_dim), "dev_1", axis=0, tiled=True)
+    all_rows = exchange_gather(arrived.reshape(-1, model_dim), "dev_1", 0)
     hid_units = gate_weight.shape[2]
     both_act = jnp.dot(all_rows, both_weight, preferred_element_type=jnp.float32)
     hidden = (jax.nn.silu(both_act[:, :hid_units]) * both_act[:, hid_units:]).astype(jnp.bfloat16)

time: 270 us -> 309 us (1.14)
  blocking collectives: 49.4 us -> 145 us
  waiting for transfers between devices: 145 us -> 91.6 us
    all_to_all x0 -> x1, blocking collectives: none -> 96 us  [exchange_gather(): parts = lax.all_to_all(parts, axis, split_axis=0, concat_axis=0)]
    all_gather x1 -> x0, waiting for transfers between devices: 48.8 us -> none  [shards(): lax.all_gather(arrived.reshape(-1, model_dim), 'dev_1', axis=0, tiled=True)]
    reduce_scatter x1, waiting for transfers between devices: 56.8 us -> 52.4 us  [shards(): lax.psum_scatter(partial_down.astype(jnp.bfloat16), 'dev_1', scatter_dime...]
  transfers between devices with their start and end apart: 6 -> 5, of which waited for: 5 -> 4; matrix products, arithmetic and copies ran while one was open for 3% -> 3% of each run, Pallas kernels for 0% -> 0%
where the time goes in v1:
time: 309 us; the launch traced here: 308 us
  blocking collectives  145 us (47%)
  waiting for transfers between devices  91.6 us (30%)
  starting transfers between devices  32.3 us (10%)
  between operations  13.8 us (4%)
  matrix products  10.3 us (3%)
  local copies, waits for them, and re-layouts  8.33 us (3%)
  other arithmetic  6.78 us (2%)
    all_to_all x1, blocking collectives, exchange_gather(): parts = lax.all_to_all(parts, axis, split_axis=0, concat_axis=0)  96 us
    reduce_scatter x1, waiting for transfers between devices, shards(): lax.psum_scatter(partial_down.astype(jnp.bfloat16), 'dev_1', scatter_dime...  52.4 us
    all_gather x1, blocking collectives, side_by_side(): lax.all_gather(both, axis, axis=dim, tiled=True)  25.4 us
    all_to_all x1, blocking collectives, shards(): lax.all_to_all(outgoing.reshape(experts * x_count, slot_cap, model_dim),...  23.7 us
    all_to_all x1, waiting for transfers between devices, shards(): lax.all_to_all(summed.reshape(experts * x_count, slot_cap, model_dim), ('...  16.8 us
    all_to_all x1, waiting for transfers between devices, shards(): lax.all_to_all(payload.reshape(x_count, y_count, block_rows, payload.shap...  12.6 us
    all_to_all x1, starting transfers between devices, shards(): lax.all_to_all(summed.reshape(experts * x_count, slot_cap, model_dim), ('...  11 us
    all_to_all x1, starting transfers between devices, shards(): lax.all_to_all(out_proj.reshape(dev_count, -1, out_proj.shape[1]), DEV, 0...  10.5 us
  transfers between devices with their start and end apart: 5, of which 4 were waited for; matrix products, arithmetic and copies ran while one was open for 3% of the time, Pallas kernels for 0%

profile of v1, /device:TPU:1, one launch (start us, length us, event | category | flops | bytes accessed | tf_op | source)
XLA Modules:
  0.0 308.2 jit_solution(9852712527240722028)
XLA Ops:
  6.5 2.1 copy_bitcast_fusion
  8.6 10.5 %all-to-all-start = ((bf16[32,128,64]{1,2,0:T(8,128)(2,1)}), bf16[32,128,64]{1,2,0:T(8,128)(2,1)S(1)}, u32[]{:S(2)}, u32[]{:S(2)}) async-start(bf16[32,128,64]{1,2,0:T(8,128)(2,1)} %copy_bitcast_fusion), calls=%async_computation | async-start | bytes 1048576 | tf_op jit(solution)/shard_map/all_to_all | solution.py:170
  19.3 0.6 reduce-window.6
  19.9 0.2 slice_reduce_fusion
  20.0 0.2 reduce-window.9
  20.3 0.2 slice_reduce_fusion.1
  20.5 0.1 copy.61
  20.7 0.2 convolution_convert_fusion.3
  21.0 0.1 pad_maximum_fusion.1
  21.1 25.4 %all_gather.3 = bf16[16,2,8193]{2,1,0:T(2,128)(2,1)S(1)} all-gather(bf16[1,2,8193]{2,1,0:T(2,128)(2,1)S(1)} %pad_maximum_fusion.1), channel_id=1, replica_groups=mesh['grp'=16,'dev_0'=4,'dev_1'=8] {'grp'}, dimensions={0}, use_global_device_ids=true | all-gather | bytes 557124 | tf_op jit(solution)/shard_map/all_gather | solution.py:23
  46.5 0.7 slice.56
  47.2 0.1 copy.74
  47.5 0.1 select_reduce_fusion.1
  47.7 0.4 reshape.237
  48.1 0.6 fusion.13
  48.7 0.2 fusion.4
  49.0 0.2 fusion.62
  49.2 0.6 fusion.3
  49.8 0.1 copy.66
  50.0 0.3 concatenate.28
  50.3 1.5 convolution_convert_fusion
  51.9 4.4 %all-to-all-start.1 = ((bf16[4,8,8,2176]{3,2,1,0:T(8,128)(2,1)}), bf16[4,8,8,2176]{3,2,1,0:T(8,128)(2,1)S(1)}, u32[]{:S(2)}, u32[]{:S(2)}) async-start(bf16[4,8,8,2176]{3,2,1,0:T(8,128)(2,1)} %bitcast.16), calls=%async_computation.1 | async-start | bytes 2228224 | tf_op jit(solution)/shard_map/all_to_all | solution.py:194
  56.5 2.7 pad_maximum_fusion
  59.2 12.6 %all-to-all-done.1 = bf16[4,8,8,2176]{3,2,1,0:T(8,128)(2,1)S(1)} async-done(((bf16[4,8,8,2176]{3,2,1,0:T(8,128)(2,1)}), bf16[4,8,8,2176]{3,2,1,0:T(8,128)(2,1)S(1)}, u32[]{:S(2)}, u32[]{:S(2)}) %all-to-all-start.1) | async-done | bytes 1114144 | tf_op jit(solution)/shard_map/all_to_all | solution.py:194
  71.8 1.0 reduce_sum.87
  72.7 6.4 %all-to-all-start.2 = ((bf16[8,8,2176]{2,1,0:T(8,128)(2,1)}), bf16[8,8,2176]{2,1,0:T(8,128)(2,1)S(1)}, u32[]{:S(2)}, u32[]{:S(2)}) async-start(bf16[8,8,2176]{2,1,0:T(8,128)(2,1)} %reduce_sum.87), calls=%async_computation.2 | async-start | bytes 557056 | tf_op jit(solution)/shard_map/all_to_all | solution.py:200
  79.3 0.2 select_reduce_fusion
  79.7 9.8 %all-to-all-done.2 = bf16[8,8,2176]{2,1,0:T(8,128)(2,1)S(1)} async-done(((bf16[8,8,2176]{2,1,0:T(8,128)(2,1)}), bf16[8,8,2176]{2,1,0:T(8,128)(2,1)S(1)}, u32[]{:S(2)}, u32[]{:S(2)}) %all-to-all-start.2) | async-done | bytes 278560 | tf_op jit(solution)/shard_map/all_to_all | solution.py:200
  89.6 0.1 fusion.51
  89.7 0.2 fusion.34
  89.9 0.2 convolution_convert_fusion.2
  90.1 0.1 broadcast_in_dim.78
  90.3 0.3 broadcast_in_dim.79
  90.6 23.7 %all_to_all.30 = bf16[64,2,2048]{2,1,0:T(2,128)(2,1)S(1)} all-to-all(bf16[64,2,2048]{2,1,0:T(2,128)(2,1)S(1)} %bitcast.84), channel_id=1, replica_groups=mesh['grp'=16,'dev_0'=4,'dev_1'=8] {'grp','dev_0'}, dimensions={0} | all-to-all | bytes 1048576 | tf_op jit(solution)/shard_map/all_to_all | solution.py:223
  114.3 0.2 stack_reshape.2
  114.5 0.5 stack.3
  115.1 96.0 %all_to_all.31 = bf16[8,128,2048]{2,1,0:T(8,128)(2,1)S(1)} all-to-all(bf16[8,128,2048]{2,1,0:T(8,128)(2,1)S(1)} %stack.3), channel_id=1, replica_groups=mesh['grp'=16,'dev_0'=4,'dev_1'=8] {'dev_1'}, dimensions={0} | all-to-all | bytes 8388608 | tf_op jit(solution)/shard_map/all_to_all | solution.py:16
  211.1 2.3 fusion.63
  213.4 0.3 fusion.10
  213.8 3.2 %convolution_convert_fusion.1 = bf16[1024,2048]{1,0:T(8,128)(2,1)} fusion(bf16[1024,256]{1,0:T(8,128)(2,1)S(1)} %fusion.10, bf16[1,256,2048]{2,1,0:T(8,128)(2,1)S(1)} %copy-done), kind=kOutput, calls=%fused_computation.1 | convolution fusion | flops 1075838976 | bytes 5767168 | tf_op jit(solution)/shard_map/dot_general | solution.py:231
  217.0 52.4 %reduce-scatter.2.cloned.1.call-done = bf16[128,2048]{1,0:T(8,128)(2,1)} async-done(((bf16[1024,2048]{1,0:T(8,128)(2,1)}), bf16[128,2048]{1,0:T(8,128)(2,1)}) %reduce-scatter.2.cloned.1.call-update) | async-done | bytes 524304 | tf_op jit(solution)/shard_map/reduce_scatter | solution.py:232
  269.4 2.2 reshape.244
  271.6 11.0 %all-to-all-start.5 = ((bf16[64,2,2048]{2,1,0:T(2,128)(2,1)}), bf16[64,2,2048]{2,1,0:T(2,128)(2,1)S(1)}, u32[]{:S(2)}, u32[]{:S(2)}) async-start(bf16[64,2,2048]{2,1,0:T(2,128)(2,1)} %reshape.244), calls=%async_computation.6 | async-start | bytes 1048576 | tf_op jit(solution)/shard_map/all_to_all | solution.py:235
  282.6 0.3 select_reduce_fusion.2
  283.0 16.8 %all-to-all-done.5 = bf16[64,2,2048]{2,1,0:T(2,128)(2,1)S(1)} async-done(((bf16[64,2,2048]{2,1,0:T(2,128)(2,1)}), bf16[64,2,2048]{2,1,0:T(2,128)(2,1)S(1)}, u32[]{:S(2)}, u32[]{:S(2)}) %all-to-all-start.5) | async-done | bytes 524320 | tf_op jit(solution)/shard_map/all_to_all | solution.py:235
  299.8 0.5 convert_reduce_fusion
  300.3 0.2 reshape.245
  300.5 0.9 fusion.1
  (64 shorter events, 1.5 us)
Async XLA Ops:
  6.5 207.2 %copy-start = (bf16[1,256,2048]{2,1,0:T(8,128)(2,1)S(1)}, bf16[1,256,2048]{2,1,0:T(8,128)(2,1)}, u32[]{:S(2)}) copy-start(bf16[1,256,2048]{2,1,0:T(8,128)(2,1)} %param.31) | copy-start | bytes 3145732
  6.5 12.6 %copy-start.9 = (f32[256,2]{0,1:T(2,128)S(1)}, f32[256,2]{0,1:T(2,128)}, u32[]{:S(2)}) copy-start(f32[256,2]{0,1:T(2,128)} %param.18) | copy-start | bytes 6148
  6.5 12.6 %copy-start.12 = (f32[2]{0:T(128)S(1)}, f32[2]{0:T(128)}, u32[]{:S(2)}) copy-start(f32[2]{0:T(128)} %param.19) | copy-start | bytes 28
  6.5 14.0 %copy-start.6 = (bf16[256,128]{1,0:T(8,128)(2,1)S(1)}, bf16[256,128]{1,0:T(8,128)(2,1)}, u32[]{:S(2)}) copy-start(bf16[256,128]{1,0:T(8,128)(2,1)} %param.16) | copy-start | bytes 196612
  6.5 14.2 %copy-start.3 = (bf16[256,128]{1,0:T(8,128)(2,1)S(1)}, bf16[256,128]{1,0:T(8,128)(2,1)}, u32[]{:S(2)}) copy-start(bf16[256,128]{1,0:T(8,128)(2,1)} %param.20) | copy-start | bytes 196612
  8.6 41.4 %all-to-all-start = ((bf16[32,128,64]{1,2,0:T(8,128)(2,1)}), bf16[32,128,64]{1,2,0:T(8,128)(2,1)S(1)}, u32[]{:S(2)}, u32[]{:S(2)}) async-start(bf16[32,128,64]{1,2,0:T(8,128)(2,1)} %copy_bitcast_fusion), calls=%async_computation | async-start | bytes 1048576 | tf_op jit(solution)/shard_map/all_to_all | solution.py:170
  19.1 29.5 %copy-start.4 = (bf16[256,128]{1,0:T(8,128)(2,1)S(1)}, bf16[256,128]{1,0:T(8,128)(2,1)}, u32[]{:S(2)}) copy-start(bf16[256,128]{1,0:T(8,128)(2,1)} %param.21) | copy-start | bytes 196612
  20.9 28.2 %copy-start.14 = (f32[2]{0:T(128)S(1)}, f32[2]{0:T(128)}, u32[]{:S(2)}) copy-start(f32[2]{0:T(128)} %param.22) | copy-start | bytes 28
  47.2 2.7 copy-start.5
  47.2 2.7 copy-start.11
  51.9 4.4 %copy-start.10 = (s32[8,2]{0,1:T(2,128)S(1)}, s32[8,2]{0,1:T(2,128)}, u32[]{:S(2)}) copy-start(s32[8,2]{0,1:T(2,128)} %param.28) | copy-start | bytes 196
  51.9 4.6 %copy-start.2 = (bf16[1,2048,256]{2,1,0:T(8,128)(2,1)S(1)}, bf16[1,2048,256]{2,1,0:T(8,128)(2,1)}, u32[]{:S(2)}) copy-start(bf16[1,2048,256]{2,1,0:T(8,128)(2,1)} %param.30) | copy-start | bytes 3145732
  51.9 19.9 %all-to-all-start.1 = ((bf16[4,8,8,2176]{3,2,1,0:T(8,128)(2,1)}), bf16[4,8,8,2176]{3,2,1,0:T(8,128)(2,1)S(1)}, u32[]{:S(2)}, u32[]{:S(2)}) async-start(bf16[4,8,8,2176]{3,2,1,0:T(8,128)(2,1)} %bitcast.16), calls=%async_computation.1 | async-start | bytes 2228224 | tf_op jit(solution)/shard_map/all_to_all | solution.py:194
  59.2 30.4 %copy-start.7 = (bf16[8,2048]{1,0:T(8,128)(2,1)S(1)}, bf16[8,2048]{1,0:T(8,128)(2,1)}, u32[]{:S(2)}) copy-start(bf16[8,2048]{1,0:T(8,128)(2,1)} %param.25) | copy-start | bytes 98308
  59.2 30.7 %copy-start.8 = (f32[2048]{0:T(1024)S(1)}, f32[2048]{0:T(1024)}, u32[]{:S(2)}) copy-start(f32[2048]{0:T(1024)} %param.26) | copy-start | bytes 24580
  72.7 16.8 %all-to-all-start.2 = ((bf16[8,8,2176]{2,1,0:T(8,128)(2,1)}), bf16[8,8,2176]{2,1,0:T(8,128)(2,1)S(1)}, u32[]{:S(2)}, u32[]{:S(2)}) async-start(bf16[8,8,2176]{2,1,0:T(8,128)(2,1)} %reduce_sum.87), calls=%async_computation.2 | async-start | bytes 557056 | tf_op jit(solution)/shard_map/all_to_all | solution.py:200
  79.1 190.3 %reduce-scatter.2.cloned.1.call-start = ((), (), s32[]{:S(2)}) async-start(), calls=%async_computation.7 | async-start | bytes 4718592 | tf_op jit(solution)/shard_map/reduce_scatter | solution.py:232
  115.1 96.0 %copy-start.1 = (bf16[2048,512]{1,0:T(8,128)(2,1)S(1)}, bf16[2048,512]{1,0:T(8,128)(2,1)}, u32[]{:S(2)}) copy-start(bf16[2048,512]{1,0:T(8,128)(2,1)} %pad_maximum_fusion) | copy-start | bytes 6291460
  217.0 65.7 %copy-start.13 = (f32[2048,16]{0,1:T(8,128)S(1)}, f32[2048,16]{0,1:T(8,128)}, u32[]{:S(2)}) copy-start(f32[2048,16]{0,1:T(8,128)} %param.27) | copy-start | bytes 393220
  271.6 28.2 %all-to-all-start.5 = ((bf16[64,2,2048]{2,1,0:T(2,128)(2,1)}), bf16[64,2,2048]{2,1,0:T(2,128)(2,1)S(1)}, u32[]{:S(2)}, u32[]{:S(2)}) async-start(bf16[64,2,2048]{2,1,0:T(2,128)(2,1)} %reshape.244), calls=%async_computation.6 | async-start | bytes 1048576 | tf_op jit(solution)/shard_map/all_to_all | solution.py:235
Sparse Core Ops, SparseCore 0:
  217.1 52.2 reduce-scatter.1
